TPU v7x, 128 devices: a whole 4x4x4 slice. The times are simulated.
128 devices in a mesh: tm: 4 (over x), space: 16 (over z, y), ens: 2 (over core).
Axes of the slice: x: 4, y: 4, z: 4, core: 2. Of those that a mesh axis runs over, the one named last changes fastest.
Arguments:
- start_states: float32 [4, 16, 1024, 1024], P('tm', 'ens', 'space'), may hold values from -6 to 6
- velocity_x: float32 [1024, 1024], P('space'), may hold values from -0.15 to 0.15
- velocity_y: float32 [1024, 1024], P('space'), may hold values from -0.15 to 0.15
- diffusivity: float32 [1024, 1024], P('space'), may hold values from 0.06 to 0.2
- source_shape: float32 [1024, 1024], P('space'), may hold values from -6 to 6
- params: float32 [16, 128], P('ens'), may hold values from -6 to 6
- obs_cell: int32 [4, 1024], P('tm', 'space'), may hold values from 0 to 1048575, as said below
- obs_data: float32 [4, 1024], P('tm', 'space'), may hold values from -6 to 6
- obs_noise: float32 [4, 1024, 16], P('tm', 'space'), may hold values from -6 to 6
- obs_var: float32 [4, 1024], P('tm', 'space'), may hold values from 0.05 to 0.5
Outputs:
- new_states: float32 [4, 16, 1024, 1024], P('tm', 'ens', 'space')
- new_params: float32 [16, 128], P('ens')
Inputs may be any that keep to these rules, and one draw needn't show every extreme that they name: `obs_cell`: entry (n, o) lies in the rows of slab o // 64, that is row (o // 64) * 64 up to 63 rows further.
All inputs are finite; a program needn't handle non-finite values.
Results may differ from a plain program's by a relative error of at most 0.0003.
Values sent between devices are 32-bit elements; how exact they have to be, the bound alone decides.
No kernel may reach another device: no remote copies, remote signals or barrier semaphores. Data moves between devices by JAX's collectives and lax.ppermute only.
A program may use at most 128 MiB of HBM per device.

v0:
```python
import math
import jax
import jax.numpy as jnp
from jax import lax
from jax.sharding import PartitionSpec as P

FINE = 4
FINE_DT = 0.25


def with_halo(cells, sides, width):
    for axis, dim in sides:
        count = lax.axis_size(axis)
        ends = count - 1
        head = lax.slice_in_dim(cells, 0, width, axis=dim)
        tail = lax.slice_in_dim(cells, cells.shape[dim] - width, cells.shape[dim], axis=dim)
        cells = jnp.concatenate(
            [
                lax.ppermute(tail, axis, [(i, (i + 1) % count) for i in range(ends)]),
                cells,
                lax.ppermute(head, axis, [((i + 1) % count, i) for i in range(ends)]),
            ],
            axis=dim,
        )
    return cells


def shifted(value, axis, steps):
    count = lax.axis_size(axis)
    first, last = (max(0, -steps), min(count, count - steps))
    return lax.ppermute(value, axis, [(source, source + steps) for source in range(first, last)])


def advance(values_in, coeffs, inside, step_size, forcing):
    middle = values_in[:, 1:-1, :]
    above_row = values_in[:, :-2, :]
    below_row = values_in[:, 2:, :]
    west_cell = jnp.pad(middle[:, :, :-1], ((0, 0), (0, 0), (1, 0)))
    east_cell = jnp.pad(middle[:, :, 1:], ((0, 0), (0, 0), (0, 1)))
    spread_term = coeffs[0] * (above_row + below_row + west_cell + east_cell - 4.0 * middle)
    tendency = (
        spread_term
        - coeffs[1] * (east_cell - west_cell) * 0.5
        - coeffs[2] * (below_row - above_row) * 0.5
    )
    if forcing is not None:
        tendency = tendency + forcing
    return (middle + step_size * tendency) * inside


def row_inside(first_row, count, total_rows):
    global_rows = first_row + jnp.arange(count, dtype=jnp.int32)
    return ((global_rows >= 0) & (global_rows < total_rows)).astype(jnp.float32)[:, None]


def per_device(
    start_states,
    velocity_x,
    velocity_y,
    diffusivity,
    source_shape,
    params,
    obs_cell,
    obs_data,
    obs_noise,
    obs_var,
):
    coarse_dt = FINE_DT * FINE
    state = start_states[0]
    members_here, row_count, col_count = state.shape
    slabs = row_count * lax.axis_size("space")
    first_row = lax.axis_index("space") * row_count
    slice_index = lax.axis_index("tm")
    band_width = col_count // params.shape[1]
    spread_params = jnp.repeat(params, band_width, axis=1)
    coeffs = jnp.stack([diffusivity, velocity_x, velocity_y])
    own_rows = row_inside(first_row, row_count, slabs)
    forcing = source_shape[None] * spread_params[:, None, :]
    current = state
    coarse_part = state
    for section in range(FINE):
        padded = with_halo(current, (("space", 1),), 1)
        if section == 0:
            coarse_part = advance(padded, coeffs, own_rows, coarse_dt, None)
        current = advance(padded, coeffs, own_rows, FINE_DT, forcing)
    correction = jnp.where(slice_index > 0, current - coarse_part, current)
    running = correction
    for link in range(lax.axis_size("tm") - 1):
        earlier = shifted(running, "tm", 1)
        padded = with_halo(earlier, (("space", 1),), 1)
        running = correction + advance(padded, coeffs, own_rows, coarse_dt, None)
    new_states = running[None]
    flat = running.reshape(members_here, row_count * col_count)
    local_cell = obs_cell[0] - first_row * col_count
    predicted = jnp.take(flat, local_cell, axis=1)
    every_pred, every_param = (
        lax.all_gather(predicted, "ens", axis=0, tiled=True),
        lax.all_gather(params, "ens", axis=0, tiled=True),
    )
    total = every_pred.shape[0]
    norm_factor = 1.0 / math.sqrt(total - 1)
    inv_spread = lax.rsqrt(obs_var[0])[None, :]
    pred_mean = jnp.mean(every_pred, axis=0, keepdims=True)
    anomaly = (every_pred - pred_mean) * (inv_spread * norm_factor)
    misfit = (obs_data[0][None, :] + obs_noise[0].T - every_pred) * inv_spread
    gram = jnp.dot(anomaly, anomaly.T, precision=lax.Precision.HIGHEST)
    cross = jnp.dot(anomaly, misfit.T, precision=lax.Precision.HIGHEST)
    gram, cross = lax.psum((gram, cross), ("tm", "space"))
    system = jnp.eye(total, dtype=jnp.float32) + gram
    factor = jnp.linalg.cholesky(system)
    weights = jax.scipy.linalg.cho_solve((factor, True), cross)
    param_anom = every_param - jnp.mean(every_param, axis=0)
    own_weights = lax.dynamic_slice_in_dim(
        weights, lax.axis_index("ens") * members_here, members_here, 1
    )
    new_params = (
        params + jnp.dot(own_weights.T, param_anom, precision=lax.Precision.HIGHEST) * norm_factor
    )
    return (new_states, new_params)


def solution(mesh):
    in_specs = (
        P("tm", "ens", "space", None),
        P("space", None),
        P("space", None),
        P("space", None),
        P("space", None),
        P("ens", None),
        P("tm", "space"),
        P("tm", "space"),
        P("tm", "space", None),
        P("tm", "space"),
    )
    out_specs = (P("tm", "ens", "space", None), P("ens", None))
    return jax.shard_map(
        per_device, mesh=mesh, in_specs=in_specs, out_specs=out_specs, check_vma=False
    )
```

profile of v0, /device:TPU:0, one launch (start us, length us, event | category | flops | bytes accessed | tf_op | source)
XLA Modules:
  0.0 608.6 jit_solution(10801937823309952952)
XLA Ops:
  1.7 3.6 collective-permute-start
  6.7 5.1 fusion.52
  14.2 3.4 fusion.2
  17.7 4.5 collective-permute-start.2
  24.4 3.7 collective-permute-done.3
  30.2 3.5 collective-permute-start.4
  35.8 4.6 collective-permute-done.5
  42.6 6.0 collective-permute-start.6
  51.0 3.7 collective-permute-done.7
  54.7 4.7 subtract_select_fusion
  59.4 3.5 collective-permute-start.8
  63.0 40.2 %collective-permute-done.8 = f32[8,64,1024]{2,1,0:T(8,128)S(1)} collective-permute-done((f32[8,64,1024]{2,1,0:T(8,128)S(1)}, f32[8,64,1024]{2,1,0:T(8,128)S(1)}, u32[]{:S(2)}, u32[]{:S(2)}) %collective-permute-start.8) | collective-permute-done | bytes 2097184 | tf_op jit(solution)/shard_map/ppermute | solution.py:31
  104.5 5.2 collective-permute-start.9
  113.2 4.7 collective-permute-start.11
  117.9 38.7 %collective-permute-done.11 = f32[8,64,1024]{2,1,0:T(8,128)S(1)} collective-permute-done((f32[8,64,1024]{2,1,0:T(8,128)S(1)}, f32[8,64,1024]{2,1,0:T(8,128)S(1)}, u32[]{:S(2)}, u32[]{:S(2)}) %collective-permute-start.11) | collective-permute-done | bytes 2097184 | tf_op jit(solution)/shard_map/ppermute | solution.py:31
  156.7 3.9 collective-permute-start.12
  162.8 3.7 collective-permute-done.13
  169.5 4.5 collective-permute-start.14
  175.9 34.7 %collective-permute-done.14 = f32[8,64,1024]{2,1,0:T(8,128)S(1)} collective-permute-done((f32[8,64,1024]{2,1,0:T(8,128)}, f32[8,64,1024]{2,1,0:T(8,128)S(1)}, u32[]{:S(2)}, u32[]{:S(2)}) %collective-permute-start.14) | collective-permute-done | bytes 2097184 | tf_op jit(solution)/shard_map/ppermute | solution.py:31
  210.6 5.4 collective-permute-start.15
  218.2 5.6 collective-permute-done.16
  226.7 17.9 %copy.18 = f32[8,64,1024]{0,2,1:T(8,128)} copy(f32[8,64,1024]{2,1,0:T(8,128)} %multiply_add_fusion.4) | data formatting | bytes 4194304 | tf_op jit(solution)/shard_map/add | solution.py:91
  244.6 11.1 %gather_fusion = f32[64,8]{1,0:T(8,128)S(1)} fusion(f32[8,65536]{0,1:T(8,128)} %bitcast.43, s32[1024]{0:T(1024)S(1)} %pad_clamp_fusion), kind=kCustom, calls=%fused_computation | custom fusion | bytes 4352 | tf_op jit(solution)/shard_map/jit(_take)/gather | solution.py:95
  258.0 345.3 %all-reduce.14 = (f32[16,16]{1,0:T(8,128)S(1)}, f32[16,16]{1,0:T(8,128)S(1)}) all-reduce(f32[16,16]{1,0:T(8,128)S(1)} %fusion.21, f32[16,16]{1,0:T(8,128)S(1)} %fusion.29), channel_id=1, replica_groups=mesh['tm'=4,'space'=16,'ens'=2] {'tm','space'}, use_global_device_ids=true, to_apply=%region_4.5 | all-reduce | flops 512 | bytes 4096 | tf_op jit(solution)/shard_map/psum | solution.py:108
  (90 shorter events, 40.2 us)
Async XLA Ops:
  1.7 12.4 %collective-permute-start = (f32[8,1,1024]{2,1,0:T(1,128)S(1)}, f32[8,1,1024]{2,1,0:T(1,128)S(1)}, u32[]{:S(2)}, u32[]{:S(2)}) collective-permute-start(f32[8,1,1024]{2,1,0:T(1,128)S(1)} %get-tuple-element.31), channel_id=1, source_target_pairs={{0,2},{2,4},{4,6},{6,8},{8,10},{10,12},{12,14},{14,16},{16,18},{18... | collective-permute-start | bytes 98312 | tf_op jit(solution)/shard_map/ppermute | solution.py:19
  5.3 8.9 %collective-permute-start.1 = (f32[8,1,1024]{2,1,0:T(1,128)S(1)}, f32[8,1,1024]{2,1,0:T(1,128)S(1)}, u32[]{:S(2)}, u32[]{:S(2)}) collective-permute-start(f32[8,1,1024]{2,1,0:T(1,128)S(1)} %get-tuple-element.30), channel_id=1, source_target_pairs={{2,0},{4,2},{6,4},{8,6},{10,8},{12,10},{14,12},{16,14},{18,16},{20... | collective-permute-start | bytes 98312 | tf_op jit(solution)/shard_map/ppermute | solution.py:21
  6.6 7.6 %copy-start = (f32[1,8,64,1024]{3,2,1,0:T(8,128)S(1)}, f32[1,8,64,1024]{3,2,1,0:T(8,128)}, u32[]{:S(2)}) copy-start(f32[1,8,64,1024]{3,2,1,0:T(8,128)} %param.10) | copy-start | bytes 6291460
  17.7 6.7 %collective-permute-start.2 = (f32[8,1,1024]{2,1,0:T(1,128)S(1)}, f32[8,1,1024]{2,1,0:T(1,128)S(1)}, u32[]{:S(2)}, u32[]{:S(2)}) collective-permute-start(f32[8,1,1024]{2,1,0:T(1,128)S(1)} %get-tuple-element.25), channel_id=1, source_target_pairs={{0,2},{2,4},{4,6},{6,8},{8,10},{10,12},{12,14},{14,16},{16,18},{18... | collective-permute-start | bytes 98312 | tf_op jit(solution)/shard_map/ppermute | solution.py:19
  22.3 5.8 collective-permute-start.3
  30.2 5.6 collective-permute-start.4
  33.7 6.8 %collective-permute-start.5 = (f32[8,1,1024]{2,1,0:T(1,128)S(1)}, f32[8,1,1024]{2,1,0:T(1,128)S(1)}, u32[]{:S(2)}, u32[]{:S(2)}) collective-permute-start(f32[8,1,1024]{2,1,0:T(1,128)S(1)} %get-tuple-element.20), channel_id=1, source_target_pairs={{2,0},{4,2},{6,4},{8,6},{10,8},{12,10},{14,12},{16,14},{18,16},{20... | collective-permute-start | bytes 98312 | tf_op jit(solution)/shard_map/ppermute | solution.py:21
  42.6 8.5 %collective-permute-start.6 = (f32[8,1,1024]{2,1,0:T(1,128)S(1)}, f32[8,1,1024]{2,1,0:T(1,128)S(1)}, u32[]{:S(2)}, u32[]{:S(2)}) collective-permute-start(f32[8,1,1024]{2,1,0:T(1,128)S(1)} %get-tuple-element.17), channel_id=1, source_target_pairs={{0,2},{2,4},{4,6},{6,8},{8,10},{10,12},{12,14},{14,16},{16,18},{18... | collective-permute-start | bytes 98312 | tf_op jit(solution)/shard_map/ppermute | solution.py:19
  48.6 6.1 collective-permute-start.7
  59.4 107.1 %copy-start.1 = (f32[8,64,1024]{2,1,0:T(8,128)}, f32[8,64,1024]{2,1,0:T(8,128)S(1)}, u32[]{:S(2)}) copy-start(f32[8,64,1024]{2,1,0:T(8,128)S(1)} %subtract_select_fusion) | copy-start | bytes 6291460
  59.4 43.7 %collective-permute-start.8 = (f32[8,64,1024]{2,1,0:T(8,128)S(1)}, f32[8,64,1024]{2,1,0:T(8,128)S(1)}, u32[]{:S(2)}, u32[]{:S(2)}) collective-permute-start(f32[8,64,1024]{2,1,0:T(8,128)S(1)} %subtract_select_fusion), channel_id=1, source_target_pairs={{0,32},{32,64},{64,96},{1,33},{33,65},{65,97},{2,34},{34,66},{66,9... | collective-permute-start | bytes 6291464 | tf_op jit(solution)/shard_map/ppermute | solution.py:31
  103.2 7.3 %collective-permute-start.10 = (f32[8,1,1024]{2,1,0:T(1,128)S(1)}, f32[8,1,1024]{2,1,0:T(1,128)S(1)}, u32[]{:S(2)}, u32[]{:S(2)}) collective-permute-start(f32[8,1,1024]{2,1,0:T(1,128)S(1)} %get-tuple-element.12), channel_id=1, source_target_pairs={{2,0},{4,2},{6,4},{8,6},{10,8},{12,10},{14,12},{16,14},{18,16},{20... | collective-permute-start | bytes 98312 | tf_op jit(solution)/shard_map/ppermute | solution.py:21
  104.5 6.8 %collective-permute-start.9 = (f32[8,1,1024]{2,1,0:T(1,128)S(1)}, f32[8,1,1024]{2,1,0:T(1,128)S(1)}, u32[]{:S(2)}, u32[]{:S(2)}) collective-permute-start(f32[8,1,1024]{2,1,0:T(1,128)S(1)} %get-tuple-element.13), channel_id=1, source_target_pairs={{0,2},{2,4},{4,6},{6,8},{8,10},{10,12},{12,14},{14,16},{16,18},{18... | collective-permute-start | bytes 98312 | tf_op jit(solution)/shard_map/ppermute | solution.py:19
  113.2 43.4 %collective-permute-start.11 = (f32[8,64,1024]{2,1,0:T(8,128)S(1)}, f32[8,64,1024]{2,1,0:T(8,128)S(1)}, u32[]{:S(2)}, u32[]{:S(2)}) collective-permute-start(f32[8,64,1024]{2,1,0:T(8,128)S(1)} %multiply_add_fusion.6), channel_id=1, source_target_pairs={{0,32},{32,64},{64,96},{1,33},{33,65},{65,97},{2,34},{34,66},{66,9... | collective-permute-start | bytes 6291464 | tf_op jit(solution)/shard_map/ppermute | solution.py:31
  156.7 6.1 collective-permute-start.12
  160.7 5.8 collective-permute-start.13
  166.5 9.3 %copy-start.12 = (s32[1,64]{1,0:T(1,128)S(1)}, s32[1,64]{1,0:T(1,128)}, u32[]{:S(2)}) copy-start(s32[1,64]{1,0:T(1,128)} %param.16) | copy-start | bytes 772
  166.5 9.4 %copy-start.13 = (f32[1,64]{1,0:T(1,128)S(1)}, f32[1,64]{1,0:T(1,128)}, u32[]{:S(2)}) copy-start(f32[1,64]{1,0:T(1,128)} %param.19) | copy-start | bytes 772
  169.5 41.1 %collective-permute-start.14 = (f32[8,64,1024]{2,1,0:T(8,128)}, f32[8,64,1024]{2,1,0:T(8,128)S(1)}, u32[]{:S(2)}, u32[]{:S(2)}) collective-permute-start(f32[8,64,1024]{2,1,0:T(8,128)} %multiply_add_fusion.5), channel_id=1, source_target_pairs={{0,32},{32,64},{64,96},{1,33},{33,65},{65,97},{2,34},{34,66},{66,9... | collective-permute-start | bytes 6291464 | tf_op jit(solution)/shard_map/ppermute | solution.py:31
  210.6 7.6 %collective-permute-start.15 = (f32[8,1,1024]{2,1,0:T(1,128)S(1)}, f32[8,1,1024]{2,1,0:T(1,128)S(1)}, u32[]{:S(2)}, u32[]{:S(2)}) collective-permute-start(f32[8,1,1024]{2,1,0:T(1,128)S(1)} %get-tuple-element.5), channel_id=1, source_target_pairs={{0,2},{2,4},{4,6},{6,8},{8,10},{10,12},{12,14},{14,16},{16,18},{18... | collective-permute-start | bytes 98312 | tf_op jit(solution)/shard_map/ppermute | solution.py:19
  216.0 7.8 %copy-start.2 = (f32[8,64,1024]{2,1,0:T(8,128)S(1)}, f32[8,64,1024]{2,1,0:T(8,128)}, u32[]{:S(2)}) copy-start(f32[8,64,1024]{2,1,0:T(8,128)} %copy-done.1) | copy-start | bytes 6291460
  216.1 7.8 %collective-permute-start.16 = (f32[8,1,1024]{2,1,0:T(1,128)S(1)}, f32[8,1,1024]{2,1,0:T(1,128)S(1)}, u32[]{:S(2)}, u32[]{:S(2)}) collective-permute-start(f32[8,1,1024]{2,1,0:T(1,128)S(1)} %get-tuple-element.4), channel_id=1, source_target_pairs={{2,0},{4,2},{6,4},{8,6},{10,8},{12,10},{14,12},{16,14},{18,16},{20... | collective-permute-start | bytes 98312 | tf_op jit(solution)/shard_map/ppermute | solution.py:21
  226.7 31.1 %copy-start.10 = (f32[1,64,16]{1,2,0:T(8,128)S(1)}, f32[1,64,16]{1,2,0:T(8,128)}, u32[]{:S(2)}) copy-start(f32[1,64,16]{1,2,0:T(8,128)} %param.18) | copy-start | bytes 12292
  226.7 31.1 %copy-start.11 = (f32[1,64]{1,0:T(1,128)S(1)}, f32[1,64]{1,0:T(1,128)}, u32[]{:S(2)}) copy-start(f32[1,64]{1,0:T(1,128)} %param.17) | copy-start | bytes 772
  (7 other events, 47.6 us)
where the time goes:
time: 610 us; the launch traced here: 609 us
  blocking collectives  349 us (57%)
  waiting for transfers between devices  135 us (22%)
  starting transfers between devices  54.3 us (9%)
  local copies, waits for them, and re-layouts  43 us (7%)
  other arithmetic  24.3 us (4%)
    psum x1, blocking collectives, per_device(): gram, cross = lax.psum((gram, cross), ('tm', 'space'))  345 us
    ppermute x3, waiting for transfers between devices, shifted(): lax.ppermute(value, axis, [(source, source + steps) for source in range(f...  114 us
    ppermute x7, starting transfers between devices, with_halo(): lax.ppermute(tail, axis, [(i, (i + 1) % count) for i in range(ends)])  32.1 us
    ppermute x7, waiting for transfers between devices, with_halo(): lax.ppermute(head, axis, [((i + 1) % count, i) for i in range(ends)])  21.2 us
    add x1, local copies, waits for them, and re-layouts, per_device(): running = correction + advance(padded, coeffs, own_rows, coarse_dt, None)  17.9 us
    ppermute x3, starting transfers between devices, shifted(): lax.ppermute(value, axis, [(source, source + steps) for source in range(f...  12.7 us
  transfers between devices with their start and end apart: 17, of which 9 were waited for; matrix products, arithmetic and copies ran while one was open for 2% of the time, Pallas kernels for 0%

commit v1 on v0

--- a/solution.py
+++ b/solution.py
@@ -105,7 +105,7 @@
     misfit = (obs_data[0][None, :] + obs_noise[0].T - every_pred) * inv_spread
     gram = jnp.dot(anomaly, anomaly.T, precision=lax.Precision.HIGHEST)
     cross = jnp.dot(anomaly, misfit.T, precision=lax.Precision.HIGHEST)
-    gram, cross = lax.psum((gram, cross), ("tm", "space"))
+    gram, cross = lax.psum(lax.psum((gram, cross), "space"), "tm")
     system = jnp.eye(total, dtype=jnp.float32) + gram
     factor = jnp.linalg.cholesky(system)
     weights = jax.scipy.linalg.cho_solve((factor, True), cross)

time: 610 us -> 355 us (0.58)
  blocking collectives: 349 us -> 94.6 us
    psum x1 -> x2, blocking collectives: 345 us -> 91 us  [per_device(): gram, cross = lax.psum(lax.psum((gram, cross), 'space'), 'tm')]
  transfers between devices with their start and end apart: 17 -> 17, of which waited for: 9 -> 9; matrix products, arithmetic and copies ran while one was open for 2% -> 4% of each run, Pallas kernels for 0% -> 0%
where the time goes in v1:
time: 355 us; the launch traced here: 354 us
  waiting for transfers between devices  135 us (38%)
  blocking collectives  94.6 us (27%)
  starting transfers between devices  54.3 us (15%)
  local copies, waits for them, and re-layouts  43.1 us (12%)
  other arithmetic  24.3 us (7%)
    ppermute x3, waiting for transfers between devices, shifted(): lax.ppermute(value, axis, [(source, source + steps) for source in range(f...  114 us
    psum x2, blocking collectives, per_device(): gram, cross = lax.psum(lax.psum((gram, cross), 'space'), 'tm')  91 us
    ppermute x7, starting transfers between devices, with_halo(): lax.ppermute(tail, axis, [(i, (i + 1) % count) for i in range(ends)])  32.1 us
    ppermute x7, waiting for transfers between devices, with_halo(): lax.ppermute(head, axis, [((i + 1) % count, i) for i in range(ends)])  21.2 us
    add x1, local copies, waits for them, and re-layouts, per_device(): running = correction + advance(padded, coeffs, own_rows, coarse_dt, None)  18 us
    ppermute x3, starting transfers between devices, shifted(): lax.ppermute(value, axis, [(source, source + steps) for source in range(f...  12.7 us
    gather x1, local copies, waits for them, and re-layouts, per_device(): predicted = jnp.take(flat, local_cell, axis=1)  11.1 us
    slice x7, local copies, waits for them, and re-layouts, advance(): west_cell = jnp.pad(middle[:, :, :-1], ((0, 0), (0, 0), (1, 0)))  10.1 us
  transfers between devices with their start and end apart: 17, of which 9 were waited for; matrix products, arithmetic and copies ran while one was open for 4% of the time, Pallas kernels for 0%

profile of v1, /device:TPU:0, one launch (start us, length us, event | category | flops | bytes accessed | tf_op | source)
XLA Modules:
  0.0 354.4 jit_solution(13164018722612879295)
XLA Ops:
  1.7 3.6 %collective-permute-start = (f32[8,1,1024]{2,1,0:T(1,128)S(1)}, f32[8,1,1024]{2,1,0:T(1,128)S(1)}, u32[]{:S(2)}, u32[]{:S(2)}) collective-permute-start(f32[8,1,1024]{2,1,0:T(1,128)S(1)} %get-tuple-element.33), channel_id=1, source_target_pairs={{0,2},{2,4},{4,6},{6,8},{8,10},{10,12},{12,14},{14,16},{16,18},{18... | collective-permute-start | bytes 98312 | tf_op jit(solution)/shard_map/ppermute | solution.py:19
  6.7 5.1 %fusion.52 = (f32[8,64,1023]{2,1,0:T(8,128)}, f32[8,64,1023]{2,1,0:T(8,128)}) fusion(f32[8,64,1024]{2,1,0:T(8,128)} %bitcast.40), kind=kLoop, calls=%fused_computation.96 | loop fusion | bytes 8380416 | tf_op jit(solution)/shard_map/slice | solution.py:38
  17.7 4.5 %collective-permute-start.2 = (f32[8,1,1024]{2,1,0:T(1,128)S(1)}, f32[8,1,1024]{2,1,0:T(1,128)S(1)}, u32[]{:S(2)}, u32[]{:S(2)}) collective-permute-start(f32[8,1,1024]{2,1,0:T(1,128)S(1)} %get-tuple-element.27), channel_id=1, source_target_pairs={{0,2},{2,4},{4,6},{6,8},{8,10},{10,12},{12,14},{14,16},{16,18},{18... | collective-permute-start | bytes 98312 | tf_op jit(solution)/shard_map/ppermute | solution.py:19
  24.4 3.7 %collective-permute-done.3 = f32[8,1,1024]{2,1,0:T(1,128)S(1)} collective-permute-done((f32[8,1,1024]{2,1,0:T(1,128)S(1)}, f32[8,1,1024]{2,1,0:T(1,128)S(1)}, u32[]{:S(2)}, u32[]{:S(2)}) %collective-permute-start.3) | collective-permute-done | bytes 32800 | tf_op jit(solution)/shard_map/ppermute | solution.py:21
  30.2 3.5 collective-permute-start.4
  35.8 4.6 %collective-permute-done.5 = f32[8,1,1024]{2,1,0:T(1,128)S(1)} collective-permute-done((f32[8,1,1024]{2,1,0:T(1,128)S(1)}, f32[8,1,1024]{2,1,0:T(1,128)S(1)}, u32[]{:S(2)}, u32[]{:S(2)}) %collective-permute-start.5) | collective-permute-done | bytes 32800 | tf_op jit(solution)/shard_map/ppermute | solution.py:21
  42.6 6.0 %collective-permute-start.6 = (f32[8,1,1024]{2,1,0:T(1,128)S(1)}, f32[8,1,1024]{2,1,0:T(1,128)S(1)}, u32[]{:S(2)}, u32[]{:S(2)}) collective-permute-start(f32[8,1,1024]{2,1,0:T(1,128)S(1)} %get-tuple-element.19), channel_id=1, source_target_pairs={{0,2},{2,4},{4,6},{6,8},{8,10},{10,12},{12,14},{14,16},{16,18},{18... | collective-permute-start | bytes 98312 | tf_op jit(solution)/shard_map/ppermute | solution.py:19
  51.0 3.7 %collective-permute-done.7 = f32[8,1,1024]{2,1,0:T(1,128)S(1)} collective-permute-done((f32[8,1,1024]{2,1,0:T(1,128)S(1)}, f32[8,1,1024]{2,1,0:T(1,128)S(1)}, u32[]{:S(2)}, u32[]{:S(2)}) %collective-permute-start.7) | collective-permute-done | bytes 32800 | tf_op jit(solution)/shard_map/ppermute | solution.py:21
  54.7 4.7 %subtract_select_fusion = f32[8,64,1024]{2,1,0:T(8,128)S(1)} fusion(f32[8,64,1024]{2,1,0:T(8,128)S(1)} %fusion.8, f32[8,64,1024]{2,1,0:T(8,128)S(1)} %bitcast.42, f32[8,64,1023]{2,1,0:T(8,128)S(1)} %get-tuple-element.21, f32[8,64,1023]{2,1,0:T(8,128)S(1)} %get-tuple-element.20, f32[8,1,1024]{2,1,0:T(1,128)S(1)} %collective-permute-done.6, ...), kind=kLoop, calls=%fused_computation.5 | loop fusion | flops 21495808 | bytes 15884545 | tf_op jit(solution)/shard_map/jit(_where)/select_n | solution.py:86
  59.4 3.5 collective-permute-start.8
  63.0 40.2 %collective-permute-done.8 = f32[8,64,1024]{2,1,0:T(8,128)S(1)} collective-permute-done((f32[8,64,1024]{2,1,0:T(8,128)S(1)}, f32[8,64,1024]{2,1,0:T(8,128)S(1)}, u32[]{:S(2)}, u32[]{:S(2)}) %collective-permute-start.8) | collective-permute-done | bytes 2097184 | tf_op jit(solution)/shard_map/ppermute | solution.py:31
  104.5 5.2 %collective-permute-start.9 = (f32[8,1,1024]{2,1,0:T(1,128)S(1)}, f32[8,1,1024]{2,1,0:T(1,128)S(1)}, u32[]{:S(2)}, u32[]{:S(2)}) collective-permute-start(f32[8,1,1024]{2,1,0:T(1,128)S(1)} %get-tuple-element.15), channel_id=1, source_target_pairs={{0,2},{2,4},{4,6},{6,8},{8,10},{10,12},{12,14},{14,16},{16,18},{18... | collective-permute-start | bytes 98312 | tf_op jit(solution)/shard_map/ppermute | solution.py:19
  113.2 4.7 %collective-permute-start.11 = (f32[8,64,1024]{2,1,0:T(8,128)S(1)}, f32[8,64,1024]{2,1,0:T(8,128)S(1)}, u32[]{:S(2)}, u32[]{:S(2)}) collective-permute-start(f32[8,64,1024]{2,1,0:T(8,128)S(1)} %multiply_add_fusion.6), channel_id=1, source_target_pairs={{0,32},{32,64},{64,96},{1,33},{33,65},{65,97},{2,34},{34,66},{66,9... | collective-permute-start | bytes 6291464 | tf_op jit(solution)/shard_map/ppermute | solution.py:31
  118.0 38.7 %collective-permute-done.11 = f32[8,64,1024]{2,1,0:T(8,128)S(1)} collective-permute-done((f32[8,64,1024]{2,1,0:T(8,128)S(1)}, f32[8,64,1024]{2,1,0:T(8,128)S(1)}, u32[]{:S(2)}, u32[]{:S(2)}) %collective-permute-start.11) | collective-permute-done | bytes 2097184 | tf_op jit(solution)/shard_map/ppermute | solution.py:31
  156.7 3.9 %collective-permute-start.12 = (f32[8,1,1024]{2,1,0:T(1,128)S(1)}, f32[8,1,1024]{2,1,0:T(1,128)S(1)}, u32[]{:S(2)}, u32[]{:S(2)}) collective-permute-start(f32[8,1,1024]{2,1,0:T(1,128)S(1)} %get-tuple-element.11), channel_id=1, source_target_pairs={{0,2},{2,4},{4,6},{6,8},{8,10},{10,12},{12,14},{14,16},{16,18},{18... | collective-permute-start | bytes 98312 | tf_op jit(solution)/shard_map/ppermute | solution.py:19
  162.8 3.7 %collective-permute-done.13 = f32[8,1,1024]{2,1,0:T(1,128)S(1)} collective-permute-done((f32[8,1,1024]{2,1,0:T(1,128)S(1)}, f32[8,1,1024]{2,1,0:T(1,128)S(1)}, u32[]{:S(2)}, u32[]{:S(2)}) %collective-permute-start.13) | collective-permute-done | bytes 32800 | tf_op jit(solution)/shard_map/ppermute | solution.py:21
  169.5 4.5 %collective-permute-start.14 = (f32[8,64,1024]{2,1,0:T(8,128)}, f32[8,64,1024]{2,1,0:T(8,128)S(1)}, u32[]{:S(2)}, u32[]{:S(2)}) collective-permute-start(f32[8,64,1024]{2,1,0:T(8,128)} %multiply_add_fusion.5), channel_id=1, source_target_pairs={{0,32},{32,64},{64,96},{1,33},{33,65},{65,97},{2,34},{34,66},{66,9... | collective-permute-start | bytes 6291464 | tf_op jit(solution)/shard_map/ppermute | solution.py:31
  175.9 34.7 %collective-permute-done.14 = f32[8,64,1024]{2,1,0:T(8,128)S(1)} collective-permute-done((f32[8,64,1024]{2,1,0:T(8,128)}, f32[8,64,1024]{2,1,0:T(8,128)S(1)}, u32[]{:S(2)}, u32[]{:S(2)}) %collective-permute-start.14) | collective-permute-done | bytes 2097184 | tf_op jit(solution)/shard_map/ppermute | solution.py:31
  210.6 5.4 %collective-permute-start.15 = (f32[8,1,1024]{2,1,0:T(1,128)S(1)}, f32[8,1,1024]{2,1,0:T(1,128)S(1)}, u32[]{:S(2)}, u32[]{:S(2)}) collective-permute-start(f32[8,1,1024]{2,1,0:T(1,128)S(1)} %get-tuple-element.7), channel_id=1, source_target_pairs={{0,2},{2,4},{4,6},{6,8},{8,10},{10,12},{12,14},{14,16},{16,18},{18... | collective-permute-start | bytes 98312 | tf_op jit(solution)/shard_map/ppermute | solution.py:19
  218.2 5.6 %collective-permute-done.16 = f32[8,1,1024]{2,1,0:T(1,128)S(1)} collective-permute-done((f32[8,1,1024]{2,1,0:T(1,128)S(1)}, f32[8,1,1024]{2,1,0:T(1,128)S(1)}, u32[]{:S(2)}, u32[]{:S(2)}) %collective-permute-start.16) | collective-permute-done | bytes 32800 | tf_op jit(solution)/shard_map/ppermute | solution.py:21
  226.7 18.0 %copy.18 = f32[8,64,1024]{0,2,1:T(8,128)} copy(f32[8,64,1024]{2,1,0:T(8,128)} %multiply_add_fusion.4) | data formatting | bytes 4194304 | tf_op jit(solution)/shard_map/add | solution.py:91
  244.7 11.1 %gather_fusion = f32[64,8]{1,0:T(8,128)S(1)} fusion(f32[8,65536]{0,1:T(8,128)} %bitcast.43, s32[1024]{0:T(1024)S(1)} %pad_clamp_fusion), kind=kCustom, calls=%fused_computation | custom fusion | bytes 4352 | tf_op jit(solution)/shard_map/jit(_take)/gather | solution.py:95
  258.1 73.2 %all-reduce.14 = (f32[16,16]{1,0:T(8,128)S(1)}, f32[16,16]{1,0:T(8,128)S(1)}) all-reduce(f32[16,16]{1,0:T(8,128)S(1)} %fusion.21, f32[16,16]{1,0:T(8,128)S(1)} %fusion.29), channel_id=1, replica_groups=mesh['tm'=4,'space'=16,'ens'=2] {'space'}, use_global_device_ids=true, to_apply=%region_5.6 | all-reduce | flops 512 | bytes 4096 | tf_op jit(solution)/shard_map/psum | solution.py:108
  331.3 17.8 %all-reduce.15 = (f32[16,16]{1,0:T(8,128)S(1)}, f32[16,16]{1,0:T(8,128)S(1)}) all-reduce(f32[16,16]{1,0:T(8,128)S(1)} %get-tuple-element.2, f32[16,16]{1,0:T(8,128)S(1)} %get-tuple-element.3), channel_id=1, replica_groups=mesh['tm'=4,'space'=16,'ens'=2] {'tm'}, use_global_device_ids=true, to_apply=%region_6.7 | all-reduce | flops 512 | bytes 4096 | tf_op jit(solution)/shard_map/psum | solution.py:108
  (91 shorter events, 43.6 us)
Async XLA Ops:
  1.7 12.4 %collective-permute-start = (f32[8,1,1024]{2,1,0:T(1,128)S(1)}, f32[8,1,1024]{2,1,0:T(1,128)S(1)}, u32[]{:S(2)}, u32[]{:S(2)}) collective-permute-start(f32[8,1,1024]{2,1,0:T(1,128)S(1)} %get-tuple-element.33), channel_id=1, source_target_pairs={{0,2},{2,4},{4,6},{6,8},{8,10},{10,12},{12,14},{14,16},{16,18},{18... | collective-permute-start | bytes 98312 | tf_op jit(solution)/shard_map/ppermute | solution.py:19
  5.3 8.9 %collective-permute-start.1 = (f32[8,1,1024]{2,1,0:T(1,128)S(1)}, f32[8,1,1024]{2,1,0:T(1,128)S(1)}, u32[]{:S(2)}, u32[]{:S(2)}) collective-permute-start(f32[8,1,1024]{2,1,0:T(1,128)S(1)} %get-tuple-element.32), channel_id=1, source_target_pairs={{2,0},{4,2},{6,4},{8,6},{10,8},{12,10},{14,12},{16,14},{18,16},{20... | collective-permute-start | bytes 98312 | tf_op jit(solution)/shard_map/ppermute | solution.py:21
  6.6 7.6 %copy-start = (f32[1,8,64,1024]{3,2,1,0:T(8,128)S(1)}, f32[1,8,64,1024]{3,2,1,0:T(8,128)}, u32[]{:S(2)}) copy-start(f32[1,8,64,1024]{3,2,1,0:T(8,128)} %param.10) | copy-start | bytes 6291460
  17.7 6.7 %collective-permute-start.2 = (f32[8,1,1024]{2,1,0:T(1,128)S(1)}, f32[8,1,1024]{2,1,0:T(1,128)S(1)}, u32[]{:S(2)}, u32[]{:S(2)}) collective-permute-start(f32[8,1,1024]{2,1,0:T(1,128)S(1)} %get-tuple-element.27), channel_id=1, source_target_pairs={{0,2},{2,4},{4,6},{6,8},{8,10},{10,12},{12,14},{14,16},{16,18},{18... | collective-permute-start | bytes 98312 | tf_op jit(solution)/shard_map/ppermute | solution.py:19
  22.3 5.8 %collective-permute-start.3 = (f32[8,1,1024]{2,1,0:T(1,128)S(1)}, f32[8,1,1024]{2,1,0:T(1,128)S(1)}, u32[]{:S(2)}, u32[]{:S(2)}) collective-permute-start(f32[8,1,1024]{2,1,0:T(1,128)S(1)} %get-tuple-element.26), channel_id=1, source_target_pairs={{2,0},{4,2},{6,4},{8,6},{10,8},{12,10},{14,12},{16,14},{18,16},{20... | collective-permute-start | bytes 98312 | tf_op jit(solution)/shard_map/ppermute | solution.py:21
  30.2 5.6 %collective-permute-start.4 = (f32[8,1,1024]{2,1,0:T(1,128)S(1)}, f32[8,1,1024]{2,1,0:T(1,128)S(1)}, u32[]{:S(2)}, u32[]{:S(2)}) collective-permute-start(f32[8,1,1024]{2,1,0:T(1,128)S(1)} %get-tuple-element.23), channel_id=1, source_target_pairs={{0,2},{2,4},{4,6},{6,8},{8,10},{10,12},{12,14},{14,16},{16,18},{18... | collective-permute-start | bytes 98312 | tf_op jit(solution)/shard_map/ppermute | solution.py:19
  33.7 6.8 %collective-permute-start.5 = (f32[8,1,1024]{2,1,0:T(1,128)S(1)}, f32[8,1,1024]{2,1,0:T(1,128)S(1)}, u32[]{:S(2)}, u32[]{:S(2)}) collective-permute-start(f32[8,1,1024]{2,1,0:T(1,128)S(1)} %get-tuple-element.22), channel_id=1, source_target_pairs={{2,0},{4,2},{6,4},{8,6},{10,8},{12,10},{14,12},{16,14},{18,16},{20... | collective-permute-start | bytes 98312 | tf_op jit(solution)/shard_map/ppermute | solution.py:21
  42.6 8.5 %collective-permute-start.6 = (f32[8,1,1024]{2,1,0:T(1,128)S(1)}, f32[8,1,1024]{2,1,0:T(1,128)S(1)}, u32[]{:S(2)}, u32[]{:S(2)}) collective-permute-start(f32[8,1,1024]{2,1,0:T(1,128)S(1)} %get-tuple-element.19), channel_id=1, source_target_pairs={{0,2},{2,4},{4,6},{6,8},{8,10},{10,12},{12,14},{14,16},{16,18},{18... | collective-permute-start | bytes 98312 | tf_op jit(solution)/shard_map/ppermute | solution.py:19
  48.6 6.1 %collective-permute-start.7 = (f32[8,1,1024]{2,1,0:T(1,128)S(1)}, f32[8,1,1024]{2,1,0:T(1,128)S(1)}, u32[]{:S(2)}, u32[]{:S(2)}) collective-permute-start(f32[8,1,1024]{2,1,0:T(1,128)S(1)} %get-tuple-element.18), channel_id=1, source_target_pairs={{2,0},{4,2},{6,4},{8,6},{10,8},{12,10},{14,12},{16,14},{18,16},{20... | collective-permute-start | bytes 98312 | tf_op jit(solution)/shard_map/ppermute | solution.py:21
  59.4 107.1 %copy-start.1 = (f32[8,64,1024]{2,1,0:T(8,128)}, f32[8,64,1024]{2,1,0:T(8,128)S(1)}, u32[]{:S(2)}) copy-start(f32[8,64,1024]{2,1,0:T(8,128)S(1)} %subtract_select_fusion) | copy-start | bytes 6291460
  59.4 43.7 %collective-permute-start.8 = (f32[8,64,1024]{2,1,0:T(8,128)S(1)}, f32[8,64,1024]{2,1,0:T(8,128)S(1)}, u32[]{:S(2)}, u32[]{:S(2)}) collective-permute-start(f32[8,64,1024]{2,1,0:T(8,128)S(1)} %subtract_select_fusion), channel_id=1, source_target_pairs={{0,32},{32,64},{64,96},{1,33},{33,65},{65,97},{2,34},{34,66},{66,9... | collective-permute-start | bytes 6291464 | tf_op jit(solution)/shard_map/ppermute | solution.py:31
  103.2 7.3 %collective-permute-start.10 = (f32[8,1,1024]{2,1,0:T(1,128)S(1)}, f32[8,1,1024]{2,1,0:T(1,128)S(1)}, u32[]{:S(2)}, u32[]{:S(2)}) collective-permute-start(f32[8,1,1024]{2,1,0:T(1,128)S(1)} %get-tuple-element.14), channel_id=1, source_target_pairs={{2,0},{4,2},{6,4},{8,6},{10,8},{12,10},{14,12},{16,14},{18,16},{20... | collective-permute-start | bytes 98312 | tf_op jit(solution)/shard_map/ppermute | solution.py:21
  104.5 6.8 %collective-permute-start.9 = (f32[8,1,1024]{2,1,0:T(1,128)S(1)}, f32[8,1,1024]{2,1,0:T(1,128)S(1)}, u32[]{:S(2)}, u32[]{:S(2)}) collective-permute-start(f32[8,1,1024]{2,1,0:T(1,128)S(1)} %get-tuple-element.15), channel_id=1, source_target_pairs={{0,2},{2,4},{4,6},{6,8},{8,10},{10,12},{12,14},{14,16},{16,18},{18... | collective-permute-start | bytes 98312 | tf_op jit(solution)/shard_map/ppermute | solution.py:19
  113.2 43.4 %collective-permute-start.11 = (f32[8,64,1024]{2,1,0:T(8,128)S(1)}, f32[8,64,1024]{2,1,0:T(8,128)S(1)}, u32[]{:S(2)}, u32[]{:S(2)}) collective-permute-start(f32[8,64,1024]{2,1,0:T(8,128)S(1)} %multiply_add_fusion.6), channel_id=1, source_target_pairs={{0,32},{32,64},{64,96},{1,33},{33,65},{65,97},{2,34},{34,66},{66,9... | collective-permute-start | bytes 6291464 | tf_op jit(solution)/shard_map/ppermute | solution.py:31
  156.7 6.1 %collective-permute-start.12 = (f32[8,1,1024]{2,1,0:T(1,128)S(1)}, f32[8,1,1024]{2,1,0:T(1,128)S(1)}, u32[]{:S(2)}, u32[]{:S(2)}) collective-permute-start(f32[8,1,1024]{2,1,0:T(1,128)S(1)} %get-tuple-element.11), channel_id=1, source_target_pairs={{0,2},{2,4},{4,6},{6,8},{8,10},{10,12},{12,14},{14,16},{16,18},{18... | collective-permute-start | bytes 98312 | tf_op jit(solution)/shard_map/ppermute | solution.py:19
  160.7 5.8 %collective-permute-start.13 = (f32[8,1,1024]{2,1,0:T(1,128)S(1)}, f32[8,1,1024]{2,1,0:T(1,128)S(1)}, u32[]{:S(2)}, u32[]{:S(2)}) collective-permute-start(f32[8,1,1024]{2,1,0:T(1,128)S(1)} %get-tuple-element.10), channel_id=1, source_target_pairs={{2,0},{4,2},{6,4},{8,6},{10,8},{12,10},{14,12},{16,14},{18,16},{20... | collective-permute-start | bytes 98312 | tf_op jit(solution)/shard_map/ppermute | solution.py:21
  166.5 9.3 %copy-start.12 = (s32[1,64]{1,0:T(1,128)S(1)}, s32[1,64]{1,0:T(1,128)}, u32[]{:S(2)}) copy-start(s32[1,64]{1,0:T(1,128)} %param.16) | copy-start | bytes 772
  166.5 9.4 %copy-start.13 = (f32[1,64]{1,0:T(1,128)S(1)}, f32[1,64]{1,0:T(1,128)}, u32[]{:S(2)}) copy-start(f32[1,64]{1,0:T(1,128)} %param.19) | copy-start | bytes 772
  169.5 41.1 %collective-permute-start.14 = (f32[8,64,1024]{2,1,0:T(8,128)}, f32[8,64,1024]{2,1,0:T(8,128)S(1)}, u32[]{:S(2)}, u32[]{:S(2)}) collective-permute-start(f32[8,64,1024]{2,1,0:T(8,128)} %multiply_add_fusion.5), channel_id=1, source_target_pairs={{0,32},{32,64},{64,96},{1,33},{33,65},{65,97},{2,34},{34,66},{66,9... | collective-permute-start | bytes 6291464 | tf_op jit(solution)/shard_map/ppermute | solution.py:31
  210.6 7.6 %collective-permute-start.15 = (f32[8,1,1024]{2,1,0:T(1,128)S(1)}, f32[8,1,1024]{2,1,0:T(1,128)S(1)}, u32[]{:S(2)}, u32[]{:S(2)}) collective-permute-start(f32[8,1,1024]{2,1,0:T(1,128)S(1)} %get-tuple-element.7), channel_id=1, source_target_pairs={{0,2},{2,4},{4,6},{6,8},{8,10},{10,12},{12,14},{14,16},{16,18},{18... | collective-permute-start | bytes 98312 | tf_op jit(solution)/shard_map/ppermute | solution.py:19
  216.0 7.8 %copy-start.2 = (f32[8,64,1024]{2,1,0:T(8,128)S(1)}, f32[8,64,1024]{2,1,0:T(8,128)}, u32[]{:S(2)}) copy-start(f32[8,64,1024]{2,1,0:T(8,128)} %copy-done.1) | copy-start | bytes 6291460
  216.1 7.8 %collective-permute-start.16 = (f32[8,1,1024]{2,1,0:T(1,128)S(1)}, f32[8,1,1024]{2,1,0:T(1,128)S(1)}, u32[]{:S(2)}, u32[]{:S(2)}) collective-permute-start(f32[8,1,1024]{2,1,0:T(1,128)S(1)} %get-tuple-element.6), channel_id=1, source_target_pairs={{2,0},{4,2},{6,4},{8,6},{10,8},{12,10},{14,12},{16,14},{18,16},{20... | collective-permute-start | bytes 98312 | tf_op jit(solution)/shard_map/ppermute | solution.py:21
  226.7 31.2 %copy-start.10 = (f32[1,64,16]{1,2,0:T(8,128)S(1)}, f32[1,64,16]{1,2,0:T(8,128)}, u32[]{:S(2)}) copy-start(f32[1,64,16]{1,2,0:T(8,128)} %param.18) | copy-start | bytes 12292
  226.7 31.2 %copy-start.11 = (f32[1,64]{1,0:T(1,128)S(1)}, f32[1,64]{1,0:T(1,128)}, u32[]{:S(2)}) copy-start(f32[1,64]{1,0:T(1,128)} %param.17) | copy-start | bytes 772
  (7 other events, 47.6 us)
